TPU v7x, 128 devices: a whole 4x4x4 slice. The times are simulated.
128 devices in a mesh: lat: 8 (over z, y_hi), lon: 16 (over x, y_lo, core).
Axes of the slice: x: 4, y: 4 (y_hi: 2, y_lo: 2; y = y_hi * 2 + y_lo), z: 4, core: 2. Of those that a mesh axis runs over, the one named last changes fastest.
Arguments:
- tracer: float32 [10, 768, 2048], P(None, 'lat', 'lon'), may hold values from -6 to 6
- velocity: float32 [10, 768, 2048], P(None, 'lat', 'lon'), may hold values from -6 to 6
- tracer_adjoint: float32 [10, 768, 2048], P(None, 'lat', 'lon'), may hold values from -6 to 6
- velocity_adjoint: float32 [10, 768, 2048], P(None, 'lat', 'lon'), may hold values from -6 to 6
- sea_mask: int32 [10, 768, 2048], P(None, 'lat', 'lon'), may hold values from 0 to 1, as said below
- face_east: float32 [768, 2048], P('lat', 'lon'), may hold values from 0.03 to 0.2
- face_north: float32 [768, 2048], P('lat', 'lon'), may hold values from 0.03 to 0.2
- viscosity: float32 [768, 2048], P('lat', 'lon'), may hold values from 0.1 to 0.7
- conv_first: float32 [3, 32, 20], replicated, may hold values from -0.75 to 0.75
- conv_middle: float32 [3, 32, 32], replicated, may hold values from -0.625 to 0.625
- conv_last: float32 [3, 20, 32], replicated, may hold values from -0.625 to 0.625
Outputs:
- tracer_grad: float32 [10, 768, 2048], P(None, 'lat', 'lon')
- velocity_grad: float32 [10, 768, 2048], P(None, 'lat', 'lon')
- first_grad: float32 [3, 32, 20], replicated
- middle_grad: float32 [3, 32, 32], replicated
- last_grad: float32 [3, 20, 32], replicated
Inputs may be any that keep to these rules, and one draw needn't show every extreme that they name: `sea_mask`: in each column a cell is sea from the top level down to the column's depth and land below it; a depth may be zero (a land column).
All inputs are finite; a program needn't handle non-finite values.
Results may differ from a plain program's by a relative error of at most 0.00015.
Values sent between devices are 32-bit elements; how exact they have to be, the bound alone decides.
No kernel may reach another device: no remote copies, remote signals or barrier semaphores. Data moves between devices by JAX's collectives and lax.ppermute only.
A program may use at most 128 MiB of HBM per device.

v0:
```python
import math
import jax
import jax.numpy as jnp
from jax import lax
from jax.sharding import PartitionSpec as P

KW = 3
highest = lax.Precision.HIGHEST


def with_halo(block, sides, width):
    for axis, dim in sides:
        count = lax.axis_size(axis)
        forward = [(i, i + 1) for i in range(count - 1)]
        forward.append((count - 1, 0))
        backward = [(target, source) for source, target in forward]
        low = lax.ppermute(
            lax.slice_in_dim(block, block.shape[dim] - width, None, axis=dim), axis, forward
        )
        high = lax.ppermute(lax.slice_in_dim(block, 0, width, axis=dim), axis, backward)
        block = jnp.concatenate([low, block, high], axis=dim)
    return block


def laplace(values, sea_pad, east_pad, north_pad):
    centre = values[..., 1:-1, 1:-1]
    sea_centre = sea_pad[..., 1:-1, 1:-1]
    summed = (
        east_pad[1:-1, 1:-1]
        * sea_centre
        * sea_pad[..., 1:-1, 2:]
        * (values[..., 1:-1, 2:] - centre)
    )
    summed = summed + east_pad[1:-1, :-2] * sea_pad[..., 1:-1, :-2] * sea_centre * (
        values[..., 1:-1, :-2] - centre
    )
    summed = summed + north_pad[1:-1, 1:-1] * sea_centre * sea_pad[..., 2:, 1:-1] * (
        values[..., 2:, 1:-1] - centre
    )
    summed = summed + north_pad[:-2, 1:-1] * sea_pad[..., :-2, 1:-1] * sea_centre * (
        values[..., :-2, 1:-1] - centre
    )
    return summed


def domain_rows(tile_rows, margin):
    start = lax.axis_index("lat") * tile_rows - margin
    global_row = start + jnp.arange(tile_rows + 2 * margin, dtype=jnp.int32)
    total_rows = tile_rows * lax.axis_size("lat")
    return ((global_row >= 0) & (global_row < total_rows)).astype(jnp.float32)[:, None]


def periodic_conv(kernel, values):
    summed = jnp.zeros((kernel.shape[1],) + values.shape[1:], jnp.float32)
    for offset in range(KW):
        shifted = jnp.roll(values, 1 - offset, axis=-1)
        summed = summed + jnp.einsum("oc,cyx->oyx", kernel[offset], shifted, precision=highest)
    return summed


def network(weights, values, convolve):
    hidden = jnp.tanh(convolve(weights[0], values))
    hidden = jnp.tanh(convolve(weights[1], hidden))
    return convolve(weights[2], hidden)


def periodic_network(weights, values):
    return network(weights, values, periodic_conv)


PACKED_ROWS = 128
LANES = 128


def pack(parts):
    flat = jnp.concatenate([part.reshape(-1) for part in parts])
    rows = max(PACKED_ROWS, -(-flat.shape[0] // LANES))
    flat = jnp.pad(flat, (0, rows * LANES - flat.shape[0]))
    return flat.reshape(rows, LANES)


def unpack(total, parts):
    total = total.reshape(-1)
    out, start = ([], 0)
    for part in parts:
        out.append(total[start : start + part.size].reshape(part.shape))
        start += part.size
    return out


def on_device(
    tracer,
    velocity,
    tracer_adjoint,
    velocity_adjoint,
    sea_mask,
    face_east,
    face_north,
    viscosity,
    conv_first,
    conv_middle,
    conv_last,
):
    levels = tracer.shape[0]
    tile_rows = tracer.shape[1]
    tile_cols = tracer.shape[2]
    sea_cells = sea_mask.astype(jnp.float32)
    planes = jnp.concatenate(
        [tracer_adjoint, velocity_adjoint, sea_cells, face_east[None], face_north[None]], axis=0
    )
    padded = with_halo(planes, (("lat", 1), ("lon", 2)), 1)
    weights = (conv_first, conv_middle, conv_last)
    inputs = jnp.concatenate([tracer, velocity], axis=0)
    masked_adjoint = jnp.concatenate(
        [tracer_adjoint * sea_cells, velocity_adjoint * sea_cells], axis=0
    )
    stacked = jnp.concatenate([inputs, masked_adjoint], axis=0)
    band = lax.all_to_all(stacked, "lon", split_axis=1, concat_axis=2, tiled=True)
    closure_out, pullback = jax.vjp(periodic_network, weights, band[: 2 * levels])
    weight_grads, band_grad = pullback(band[2 * levels :])
    packed = pack(weight_grads)
    packed, padded = lax.optimization_barrier((packed, padded))
    summed = unpack(lax.psum(packed, ("lat", "lon")), weight_grads)
    input_grad = lax.all_to_all(band_grad, "lon", split_axis=2, concat_axis=1, tiled=True)
    sea_pad = padded[2 * levels : 3 * levels] * domain_rows(tile_rows, 1)
    east_pad = padded[3 * levels]
    north_pad = padded[3 * levels + 1]
    tracer_term = laplace(padded[:levels], sea_pad, east_pad, north_pad)
    first_laplace = laplace(padded[levels : 2 * levels], sea_pad, east_pad, north_pad)
    scaled = viscosity * first_laplace
    scaled_pad = with_halo(scaled, (("lat", 1), ("lon", 2)), 1)
    viscous_term = laplace(scaled_pad, sea_pad, east_pad, north_pad)
    scale = 1.0 / math.sqrt(tile_rows * lax.axis_size("lat") * tile_cols * lax.axis_size("lon"))
    tracer_grad = tracer_adjoint + tracer_term + input_grad[:levels]
    velocity_grad = velocity_adjoint - viscous_term + input_grad[levels:]
    return (tracer_grad, velocity_grad, summed[0] * scale, summed[1] * scale, summed[2] * scale)


def solution(mesh):
    return jax.shard_map(
        on_device,
        mesh=mesh,
        in_specs=(
            P(None, "lat", "lon"),
            P(None, "lat", "lon"),
            P(None, "lat", "lon"),
            P(None, "lat", "lon"),
            P(None, "lat", "lon"),
            P("lat", "lon"),
            P("lat", "lon"),
            P("lat", "lon"),
            P(),
            P(),
            P(),
        ),
        out_specs=(P(None, "lat", "lon"), P(None, "lat", "lon"), P(), P(), P()),
        check_vma=False,
    )
```

profile of v0, /device:TPU:1, one launch (start us, length us, event | category | flops | bytes accessed | tf_op | source)
XLA Modules:
  0.0 341.4 jit_solution(16073828188655921510)
XLA Ops:
  13.2 6.8 %all-to-all-start = ((f32[40,96,128]{2,0,1:T(8,128)}), f32[40,96,128]{2,0,1:T(8,128)S(1)}, u32[]{:S(2)}, u32[]{:S(2)}) async-start(f32[40,96,128]{2,0,1:T(8,128)} %copy.168), calls=%async_computation | async-start | bytes 3932160 | tf_op jit(solution)/shard_map/all_to_all | solution.py:118
  22.3 2.6 collective-permute-start
  24.9 3.5 %collective-permute-start.1 = (f32[32,1,128]{2,1,0:T(1,128)}, f32[32,1,128]{2,1,0:T(1,128)}, u32[]{:S(2)}, u32[]{:S(2)}) collective-permute-start(f32[32,1,128]{2,1,0:T(1,128)} %get-tuple-element.51), channel_id=1, source_target_pairs={{16,0},{32,16},{48,32},{64,48},{80,64},{96,80},{112,96},{0,112},{1... | collective-permute-start | bytes 49160 | tf_op jit(solution)/shard_map/ppermute | solution.py:20
  28.4 6.7 %collective-permute-done = f32[32,1,128]{2,1,0:T(1,128)S(1)} collective-permute-done((f32[32,1,128]{2,1,0:T(1,128)}, f32[32,1,128]{2,1,0:T(1,128)S(1)}, u32[]{:S(2)}, u32[]{:S(2)}) %collective-permute-start) | collective-permute-done | bytes 16416 | tf_op jit(solution)/shard_map/ppermute | solution.py:17
  38.3 2.6 copy.175
  41.0 7.2 %collective-permute-start.2 = (f32[32,98,1]{1,0,2:T(8,128)}, f32[32,98,1]{1,0,2:T(8,128)}, u32[]{:S(2)}, u32[]{:S(2)}) collective-permute-start(f32[32,98,1]{1,0,2:T(8,128)} %copy.175), channel_id=1, source_target_pairs={{0,1},{1,2},{2,3},{3,4},{4,5},{5,6},{6,7},{7,8},{8,9},{9,10},{10,1... | collective-permute-start | bytes 37640 | tf_op jit(solution)/shard_map/ppermute | solution.py:17
  48.2 2.6 copy.176
  51.5 2.5 copy.177
  54.4 2.6 copy.178
  57.0 5.2 %pad_maximum_fusion = f32[32,98,130]{2,1,0:T(8,128)} fusion(f32[32,98,1]{2,1,0:T(8,128)} %copy.178, f32[32,1,128]{2,1,0:T(1,128)} %collective-permute-done.1, f32[32,96,128]{2,1,0:T(8,128)S(1)} %bitcast_dynamic-update-slice_fusion, f32[32,1,128]{2,1,0:T(1,128)S(1)} %collective-permute-done, f32[32,98,1]{2,1,0:T(8,128)} %copy.177), kind=kLoop, calls=%fused_computation | loop fusion | flops 1630720 | bytes 3261440 | tf_op jit(solution)/shard_map/concatenate | solution.py:21
  105.6 2.5 convolution_bitcast_fusion.8
  109.8 2.9 fusion.28
  119.9 3.7 %fusion.11 = f32[20,6,2048]{2,0,1:T(8,128)} fusion(f32[32,6,2048]{2,0,1:T(8,128)S(1)} %fusion.2, f32[20,6,1]{2,0,1:T(8,128)S(1)} %slice-done.1, f32[20,6,2047]{2,0,1:T(8,128)} %split.66, f32[20,6,2047]{2,0,1:T(8,128)S(1)} %bitcast.174, f32[20,6,1]{2,0,1:T(8,128)S(1)} %split.64, f32[3,32,20]{1,2,0:T(8,128)} %param.19), kind=kOutput, calls=%fused_computation.24 | convolution fusion | flops 95354880 | bytes 4731360 | tf_op jit(solution)/shard_map/transpose(jvp(oc,cyx->oyx))/dot_general | solution.py:57
  123.6 6.0 %copy.185 = f32[20,6,2048]{0,1,2:T(8,128)} copy(f32[20,6,2048]{2,0,1:T(8,128)} %fusion.11) | data formatting | bytes 1966080 | tf_op jit(solution)/shard_map/transpose(jvp())/add_any | solution.py:56
  129.7 7.3 %reshape.80 = f32[16,1,15360]{2,1,0:T(1,128)} reshape(f32[2048,6,20]{2,1,0:T(8,128)} %bitcast.168) | data formatting | bytes 1966080
  137.0 14.4 %all-to-all-start.1 = ((f32[16,1,15360]{2,1,0:T(1,128)}), f32[16,1,15360]{2,1,0:T(1,128)}, u32[]{:S(2)}, u32[]{:S(2)}) async-start(f32[16,1,15360]{2,1,0:T(1,128)} %reshape.80), calls=%async_computation.1 | async-start | bytes 1966080 | tf_op jit(solution)/shard_map/all_to_all | solution.py:124
  151.4 5.4 %add_multiply_fusion = (f32[10,96,128]{2,1,0:T(8,128)S(1)}, f32[10,96,128]{2,1,0:T(8,128)}, f32[10,96,128]{2,1,0:T(8,128)}, f32[10,96,128]{2,1,0:T(8,128)}, f32[10,96,128]{2,1,0:T(8,128)}) fusion(f32[32,98,130]{2,1,0:T(8,128)S(1)} %copy-done.4, f32[96,128]{1,0:T(8,128)} %param.18, f32[10,98,130]{2,1,0:T(8,128)} %slice_multiply_fusion, ...), kind=kLoop, calls=%fused_computation.82 | loop fusion | flops 2457600 | bytes 7618560 | tf_op jit(solution)/shard_map/mul | solution.py:130
  157.8 5.1 %collective-permute-start.5 = (f32[10,1,128]{2,1,0:T(1,128)S(1)}, f32[10,1,128]{2,1,0:T(1,128)S(1)}, u32[]{:S(2)}, u32[]{:S(2)}) collective-permute-start(f32[10,1,128]{2,1,0:T(1,128)S(1)} %get-tuple-element.68), channel_id=1, source_target_pairs={{16,0},{32,16},{48,32},{64,48},{80,64},{96,80},{112,96},{0,112},{1... | collective-permute-start | bytes 15368 | tf_op jit(solution)/shard_map/ppermute | solution.py:20
  174.4 125.9 %all-reduce.24.cloned.1.call-done = f32[128,128]{1,0:T(8,128)} async-done(((f32[128,128]{1,0:T(8,128)}), f32[128,128]{1,0:T(8,128)}) %all-reduce.24.cloned.1.call-update) | async-done | bytes 65552 | tf_op jit(solution)/shard_map/psum | solution.py:123
  304.5 5.2 %reduce = f32[16,15360]{1,0:T(8,128)} reduce(f32[16,1,15360]{2,1,0:T(1,128)} %all-to-all-done.1, f32[]{:T(128)} %broadcast.81), dimensions={1}, to_apply=%all_to_all.25.reduce_sub_computation | reduce | bytes 1966084 | tf_op jit(solution)/shard_map/all_to_all | solution.py:124
  309.7 7.2 %reshape.81 = f32[2048,6,20]{2,1,0:T(8,128)} reshape(f32[16,15360]{1,0:T(8,128)} %reduce) | data formatting | bytes 1966080
  316.8 6.4 %copy.186 = f32[20,6,16,128]{3,1,2,0:T(8,128)} copy(f32[20,6,16,128]{0,1,3,2:T(8,128)} %bitcast.169) | data formatting | bytes 1966080 | tf_op jit(solution)/shard_map/all_to_all | solution.py:124
  323.2 2.5 fusion.98
  329.6 3.3 add_add_fusion
  (174 shorter events, 86.3 us)
Async XLA Ops:
  13.2 49.0 %all-to-all-start = ((f32[40,96,128]{2,0,1:T(8,128)}), f32[40,96,128]{2,0,1:T(8,128)S(1)}, u32[]{:S(2)}, u32[]{:S(2)}) async-start(f32[40,96,128]{2,0,1:T(8,128)} %copy.168), calls=%async_computation | async-start | bytes 3932160 | tf_op jit(solution)/shard_map/all_to_all | solution.py:118
  22.3 12.8 %collective-permute-start = (f32[32,1,128]{2,1,0:T(1,128)}, f32[32,1,128]{2,1,0:T(1,128)S(1)}, u32[]{:S(2)}, u32[]{:S(2)}) collective-permute-start(f32[32,1,128]{2,1,0:T(1,128)} %get-tuple-element.50), channel_id=1, source_target_pairs={{0,16},{16,32},{32,48},{48,64},{64,80},{80,96},{96,112},{112,0},{1... | collective-permute-start | bytes 49160 | tf_op jit(solution)/shard_map/ppermute | solution.py:17
  24.9 10.2 %collective-permute-start.1 = (f32[32,1,128]{2,1,0:T(1,128)}, f32[32,1,128]{2,1,0:T(1,128)}, u32[]{:S(2)}, u32[]{:S(2)}) collective-permute-start(f32[32,1,128]{2,1,0:T(1,128)} %get-tuple-element.51), channel_id=1, source_target_pairs={{16,0},{32,16},{48,32},{64,48},{80,64},{96,80},{112,96},{0,112},{1... | collective-permute-start | bytes 49160 | tf_op jit(solution)/shard_map/ppermute | solution.py:20
  41.0 10.5 %collective-permute-start.2 = (f32[32,98,1]{1,0,2:T(8,128)}, f32[32,98,1]{1,0,2:T(8,128)}, u32[]{:S(2)}, u32[]{:S(2)}) collective-permute-start(f32[32,98,1]{1,0,2:T(8,128)} %copy.175), channel_id=1, source_target_pairs={{0,1},{1,2},{2,3},{3,4},{4,5},{5,6},{6,7},{7,8},{8,9},{9,10},{10,1... | collective-permute-start | bytes 37640 | tf_op jit(solution)/shard_map/ppermute | solution.py:17
  50.8 3.6 %collective-permute-start.3 = (f32[32,98,1]{1,0,2:T(8,128)}, f32[32,98,1]{1,0,2:T(8,128)}, u32[]{:S(2)}, u32[]{:S(2)}) collective-permute-start(f32[32,98,1]{1,0,2:T(8,128)} %copy.176), channel_id=1, source_target_pairs={{1,0},{2,1},{3,2},{4,3},{5,4},{6,5},{7,6},{8,7},{9,8},{10,9},{11,1... | collective-permute-start | bytes 37640 | tf_op jit(solution)/shard_map/ppermute | solution.py:20
  64.4 3.6 %copy-start.9 = (f32[20,6,2047]{2,0,1:T(8,128)}, f32[20,6,2047]{2,0,1:T(8,128)S(1)}, u32[]{:S(2)}) copy-start(f32[20,6,2047]{2,0,1:T(8,128)S(1)} %get-tuple-element.63) | copy-start | bytes 2947684
  64.4 3.6 %copy-start.7 = (f32[20,6,2047]{2,0,1:T(8,128)}, f32[20,6,2047]{2,0,1:T(8,128)S(1)}, u32[]{:S(2)}) copy-start(f32[20,6,2047]{2,0,1:T(8,128)S(1)} %get-tuple-element.62) | copy-start | bytes 2947684
  74.5 9.4 %copy-start = (f32[20,6,2048]{2,0,1:T(8,128)}, f32[20,6,2048]{2,0,1:T(8,128)S(1)}, u32[]{:S(2)}) copy-start(f32[20,6,2048]{2,0,1:T(8,128)S(1)} %slice.244) | copy-start | bytes 2949124
  105.6 4.0 %copy-start.13 = (f32[20,6,2048]{2,0,1:T(8,128)}, f32[20,6,2048]{2,0,1:T(8,128)S(1)}, u32[]{:S(2)}) copy-start(f32[20,6,2048]{2,0,1:T(8,128)S(1)} %convolution_bitcast_fusion.6) | copy-start | bytes 2949124
  115.9 3.9 %copy-start.14 = (f32[20,6,2048]{2,0,1:T(8,128)S(1)}, f32[20,6,2048]{2,0,1:T(8,128)}, u32[]{:S(2)}) copy-start(f32[20,6,2048]{2,0,1:T(8,128)} %convolution_bitcast_fusion.8) | copy-start | bytes 2949124
  115.9 3.9 %slice-start.1 = ((f32[20,6,2048]{2,0,1:T(8,128)}), f32[20,6,1]{2,0,1:T(8,128)S(1)}, s32[]{:S(2)}) async-start(f32[20,6,2048]{2,0,1:T(8,128)} %copy-done.13), calls=%async_computation.4 | async-start | bytes 147456 | tf_op jit(solution)/shard_map/transpose(jvp(jit(_roll_static)))/split | solution.py:56
  129.7 21.8 %copy-start.4 = (f32[32,98,130]{2,1,0:T(8,128)S(1)}, f32[32,98,130]{2,1,0:T(8,128)}, u32[]{:S(2)}) copy-start(f32[32,98,130]{2,1,0:T(8,128)} %pad_maximum_fusion) | copy-start | bytes 4892164
  137.0 167.0 %all-to-all-start.1 = ((f32[16,1,15360]{2,1,0:T(1,128)}), f32[16,1,15360]{2,1,0:T(1,128)}, u32[]{:S(2)}, u32[]{:S(2)}) async-start(f32[16,1,15360]{2,1,0:T(1,128)} %reshape.80), calls=%async_computation.1 | async-start | bytes 1966080 | tf_op jit(solution)/shard_map/all_to_all | solution.py:124
  151.4 149.0 %all-reduce.24.cloned.1.call-start = ((), (), s32[]{:S(2)}) async-start(), calls=%async_computation.2 | async-start | bytes 131072 | tf_op jit(solution)/shard_map/psum | solution.py:123
  157.7 6.2 %collective-permute-start.4 = (f32[10,1,128]{2,1,0:T(1,128)S(1)}, f32[10,1,128]{2,1,0:T(1,128)S(1)}, u32[]{:S(2)}, u32[]{:S(2)}) collective-permute-start(f32[10,1,128]{2,1,0:T(1,128)S(1)} %get-tuple-element.69), channel_id=1, source_target_pairs={{0,16},{16,32},{32,48},{48,64},{64,80},{80,96},{96,112},{112,0},{1... | collective-permute-start | bytes 15368 | tf_op jit(solution)/shard_map/ppermute | solution.py:17
  157.8 6.1 %collective-permute-start.5 = (f32[10,1,128]{2,1,0:T(1,128)S(1)}, f32[10,1,128]{2,1,0:T(1,128)S(1)}, u32[]{:S(2)}, u32[]{:S(2)}) collective-permute-start(f32[10,1,128]{2,1,0:T(1,128)S(1)} %get-tuple-element.68), channel_id=1, source_target_pairs={{16,0},{32,16},{48,32},{64,48},{80,64},{96,80},{112,96},{0,112},{1... | collective-permute-start | bytes 15368 | tf_op jit(solution)/shard_map/ppermute | solution.py:20
  167.3 4.7 %collective-permute-start.6 = (f32[10,98,1]{1,2,0:T(1,128)S(1)}, f32[10,98,1]{1,2,0:T(1,128)S(1)}, u32[]{:S(2)}, u32[]{:S(2)}) collective-permute-start(f32[10,98,1]{1,2,0:T(1,128)S(1)} %copy.187), channel_id=1, source_target_pairs={{1,0},{2,1},{3,2},{4,3},{5,4},{6,5},{7,6},{8,7},{9,8},{10,9},{11,1... | collective-permute-start | bytes 11768 | tf_op jit(solution)/shard_map/ppermute | solution.py:20
  170.3 3.0 collective-permute-start.7
  329.6 3.4 copy-start.22
  329.6 3.4 copy-start.23
  329.6 3.4 copy-start.24
  329.6 3.4 copy-start.25
  329.6 3.4 copy-start.26
  329.6 3.4 copy-start.27
  (24 other events, 48.8 us)
Sparse Core Ops, SparseCore 0:
  163.0 137.3 all-reduce.23
where the time goes:
time: 347 us; the launch traced here: 341 us
  waiting for transfers between devices  134 us (39%)
  local copies, waits for them, and re-layouts  79.3 us (23%)
  starting transfers between devices  43.3 us (12%)
  matrix products  41.6 us (12%)
  other arithmetic  27.8 us (8%)
  between operations  15 us (4%)
    psum x1, waiting for transfers between devices, on_device(): summed = unpack(lax.psum(packed, ('lat', 'lon')), weight_grads)  126 us
    dot_general x24, matrix products, periodic_conv(): jnp.einsum('oc,cyx->oyx', kernel[offset], shifted, precision=highest)  41.6 us
    unnamed x76, local copies, waits for them, and re-layouts  21.2 us
    all_to_all x1, starting transfers between devices, on_device(): lax.all_to_all(band_grad, 'lon', split_axis=2, concat_axis=1, tiled=True)  14.4 us
    ppermute x4, starting transfers between devices, with_halo(): lax.ppermute(lax.slice_in_dim(block, block.shape[dim] - width, None, axis...  11.6 us
    ppermute x4, starting transfers between devices, with_halo(): lax.ppermute(lax.slice_in_dim(block, 0, width, axis=dim), axis, backward)  10.5 us
    ppermute x4, waiting for transfers between devices, with_halo(): lax.ppermute(lax.slice_in_dim(block, block.shape[dim] - width, None, axis...  8.05 us
    concatenate x3, other arithmetic, with_halo(): block = jnp.concatenate([low, block, high], axis=dim)  7.18 us
  transfers between devices with their start and end apart: 11, of which 5 were waited for; matrix products, arithmetic and copies ran while one was open for 11% of the time, Pallas kernels for 0%

commit v1 on v0

--- a/solution.py
+++ b/solution.py
@@ -121,7 +121,10 @@
     packed = pack(weight_grads)
     packed, padded = lax.optimization_barrier((packed, padded))
     summed = unpack(lax.psum(packed, ("lat", "lon")), weight_grads)
-    input_grad = lax.all_to_all(band_grad, "lon", split_axis=2, concat_axis=1, tiled=True)
+    input_grad = jnp.concatenate(
+        lax.all_to_all(jnp.stack(jnp.split(band_grad, lax.axis_size("lon"), axis=2)), "lon", 0, 0),
+        axis=1,
+    )
     sea_pad = padded[2 * levels : 3 * levels] * domain_rows(tile_rows, 1)
     east_pad = padded[3 * levels]
     north_pad = padded[3 * levels + 1]

time: 347 us -> 316 us (0.911)
  local copies, waits for them, and re-layouts: 79.3 us -> 58 us
  other arithmetic: 27.8 us -> 20.4 us
    all_to_all x2 -> x0, local copies, waits for them, and re-layouts: 6.88 us -> none  [on_device(): lax.all_to_all(band_grad, 'lon', split_axis=2, concat_axis=1, tiled=True)]
    add_any x1 -> x0, local copies, waits for them, and re-layouts: 6.03 us -> none  [periodic_conv(): shifted = jnp.roll(values, 1 - offset, axis=-1)]
    all_to_all x1 -> x0, other arithmetic: 5.16 us -> none  [on_device(): lax.all_to_all(band_grad, 'lon', split_axis=2, concat_axis=1, tiled=True)]
    unnamed x76 -> x89, local copies, waits for them, and re-layouts: 21.2 us -> 16.7 us
  transfers between devices with their start and end apart: 11 -> 11, of which waited for: 5 -> 5; matrix products, arithmetic and copies ran while one was open for 11% -> 12% of each run, Pallas kernels for 0% -> 0%
where the time goes in v1:
time: 316 us; the launch traced here: 312 us
  waiting for transfers between devices  133 us (42%)
  local copies, waits for them, and re-layouts  58 us (18%)
  starting transfers between devices  44.4 us (14%)
  matrix products  40.6 us (13%)
  other arithmetic  20.4 us (6%)
  between operations  14.9 us (5%)
    psum x1, waiting for transfers between devices, on_device(): summed = unpack(lax.psum(packed, ('lat', 'lon')), weight_grads)  125 us
    dot_general x24, matrix products, periodic_conv(): jnp.einsum('oc,cyx->oyx', kernel[offset], shifted, precision=highest)  40.6 us
    unnamed x89, local copies, waits for them, and re-layouts  16.7 us
    all_to_all x1, starting transfers between devices, on_device(): lax.all_to_all(jnp.stack(jnp.split(band_grad, lax.axis_size('lon'), axis=...  14.4 us
    ppermute x4, starting transfers between devices, with_halo(): lax.ppermute(lax.slice_in_dim(block, block.shape[dim] - width, None, axis...  12.7 us
    ppermute x4, starting transfers between devices, with_halo(): lax.ppermute(lax.slice_in_dim(block, 0, width, axis=dim), axis, backward)  10.5 us
    ppermute x4, waiting for transfers between devices, with_halo(): lax.ppermute(lax.slice_in_dim(block, block.shape[dim] - width, None, axis...  7.76 us
    concatenate x3, other arithmetic, with_halo(): block = jnp.concatenate([low, block, high], axis=dim)  7.17 us
  transfers between devices with their start and end apart: 11, of which 5 were waited for; matrix products, arithmetic and copies ran while one was open for 12% of the time, Pallas kernels for 0%

profile of v1, /device:TPU:1, one launch (start us, length us, event | category | flops | bytes accessed | tf_op | source)
XLA Modules:
  0.0 311.6 jit_solution(14427198269934246649)
XLA Ops:
  10.8 2.4 copy.178
  13.2 6.8 %all-to-all-start = ((f32[40,96,128]{2,0,1:T(8,128)}), f32[40,96,128]{2,0,1:T(8,128)S(1)}, u32[]{:S(2)}, u32[]{:S(2)}) async-start(f32[40,96,128]{2,0,1:T(8,128)} %copy.178), calls=%async_computation | async-start | bytes 3932160 | tf_op jit(solution)/shard_map/all_to_all | solution.py:118
  22.3 2.6 collective-permute-start
  24.9 3.5 %collective-permute-start.1 = (f32[32,1,128]{2,1,0:T(1,128)}, f32[32,1,128]{2,1,0:T(1,128)}, u32[]{:S(2)}, u32[]{:S(2)}) collective-permute-start(f32[32,1,128]{2,1,0:T(1,128)} %get-tuple-element.56), channel_id=1, source_target_pairs={{16,0},{32,16},{48,32},{64,48},{80,64},{96,80},{112,96},{0,112},{1... | collective-permute-start | bytes 49160 | tf_op jit(solution)/shard_map/ppermute | solution.py:20
  28.4 6.7 %collective-permute-done = f32[32,1,128]{2,1,0:T(1,128)S(1)} collective-permute-done((f32[32,1,128]{2,1,0:T(1,128)}, f32[32,1,128]{2,1,0:T(1,128)S(1)}, u32[]{:S(2)}, u32[]{:S(2)}) %collective-permute-start) | collective-permute-done | bytes 16416 | tf_op jit(solution)/shard_map/ppermute | solution.py:17
  36.0 2.3 fusion.108
  38.3 2.6 copy.185
  40.9 7.2 %collective-permute-start.2 = (f32[32,98,1]{1,0,2:T(8,128)}, f32[32,98,1]{1,0,2:T(8,128)}, u32[]{:S(2)}, u32[]{:S(2)}) collective-permute-start(f32[32,98,1]{1,0,2:T(8,128)} %copy.185), channel_id=1, source_target_pairs={{0,1},{1,2},{2,3},{3,4},{4,5},{5,6},{6,7},{7,8},{8,9},{9,10},{10,1... | collective-permute-start | bytes 37640 | tf_op jit(solution)/shard_map/ppermute | solution.py:17
  48.1 2.6 copy.186
  51.4 2.5 copy.187
  54.4 2.6 copy.188
  57.0 5.2 %pad_maximum_fusion = f32[32,98,130]{2,1,0:T(8,128)} fusion(f32[32,98,1]{2,1,0:T(8,128)} %copy.188, f32[32,1,128]{2,1,0:T(1,128)} %collective-permute-done.1, f32[32,96,128]{2,1,0:T(8,128)S(1)} %bitcast_dynamic-update-slice_fusion, f32[32,1,128]{2,1,0:T(1,128)S(1)} %collective-permute-done, f32[32,98,1]{2,1,0:T(8,128)} %copy.187), kind=kLoop, calls=%fused_computation | loop fusion | flops 1630720 | bytes 3261440 | tf_op jit(solution)/shard_map/concatenate | solution.py:21
  69.5 2.3 fusion.112
  89.6 2.4 fusion.2
  100.7 2.3 fusion.110
  105.6 2.4 convolution_bitcast_fusion.8
  109.8 2.9 fusion.28
  116.0 2.4 slice_multiply_fusion
  119.9 2.7 fusion.11
  132.8 14.4 %all-to-all-start.1 = ((f32[16,20,6,128]{3,1,2,0:T(8,128)}), f32[16,20,6,128]{3,1,2,0:T(8,128)}, u32[]{:S(2)}, u32[]{:S(2)}) async-start(f32[16,20,6,128]{3,1,2,0:T(8,128)} %fusion.47), calls=%async_computation.1 | async-start | bytes 2359296 | tf_op jit(solution)/shard_map/all_to_all | solution.py:125
  147.2 5.1 %add_multiply_fusion = (f32[10,96,128]{2,1,0:T(8,128)S(1)}, f32[10,96,128]{2,1,0:T(8,128)}, f32[10,96,128]{2,1,0:T(8,128)}, f32[10,96,128]{2,1,0:T(8,128)}, f32[10,96,128]{2,1,0:T(8,128)}) fusion(f32[32,98,130]{2,1,0:T(8,128)S(1)} %copy-done.4, f32[96,128]{1,0:T(8,128)} %param.18, f32[10,98,130]{2,1,0:T(8,128)} %slice_multiply_fusion, ...), kind=kLoop, calls=%fused_computation.83 | loop fusion | flops 2457600 | bytes 7618560 | tf_op jit(solution)/shard_map/mul | solution.py:133
  153.2 5.1 %collective-permute-start.5 = (f32[10,1,128]{2,1,0:T(1,128)S(1)}, f32[10,1,128]{2,1,0:T(1,128)S(1)}, u32[]{:S(2)}, u32[]{:S(2)}) collective-permute-start(f32[10,1,128]{2,1,0:T(1,128)S(1)} %get-tuple-element.73), channel_id=1, source_target_pairs={{16,0},{32,16},{48,32},{64,48},{80,64},{96,80},{112,96},{0,112},{1... | collective-permute-start | bytes 15368 | tf_op jit(solution)/shard_map/ppermute | solution.py:20
  165.9 2.8 collective-permute-start.7
  171.2 124.6 %all-reduce.24.cloned.1.call-done = f32[128,128]{1,0:T(8,128)} async-done(((f32[128,128]{1,0:T(8,128)}), f32[128,128]{1,0:T(8,128)}) %all-reduce.24.cloned.1.call-update) | async-done | bytes 65552 | tf_op jit(solution)/shard_map/psum | solution.py:123
  (182 shorter events, 80.1 us)
Async XLA Ops:
  13.2 48.9 %all-to-all-start = ((f32[40,96,128]{2,0,1:T(8,128)}), f32[40,96,128]{2,0,1:T(8,128)S(1)}, u32[]{:S(2)}, u32[]{:S(2)}) async-start(f32[40,96,128]{2,0,1:T(8,128)} %copy.178), calls=%async_computation | async-start | bytes 3932160 | tf_op jit(solution)/shard_map/all_to_all | solution.py:118
  22.3 12.8 %collective-permute-start = (f32[32,1,128]{2,1,0:T(1,128)}, f32[32,1,128]{2,1,0:T(1,128)S(1)}, u32[]{:S(2)}, u32[]{:S(2)}) collective-permute-start(f32[32,1,128]{2,1,0:T(1,128)} %get-tuple-element.55), channel_id=1, source_target_pairs={{0,16},{16,32},{32,48},{48,64},{64,80},{80,96},{96,112},{112,0},{1... | collective-permute-start | bytes 49160 | tf_op jit(solution)/shard_map/ppermute | solution.py:17
  24.9 10.2 %collective-permute-start.1 = (f32[32,1,128]{2,1,0:T(1,128)}, f32[32,1,128]{2,1,0:T(1,128)}, u32[]{:S(2)}, u32[]{:S(2)}) collective-permute-start(f32[32,1,128]{2,1,0:T(1,128)} %get-tuple-element.56), channel_id=1, source_target_pairs={{16,0},{32,16},{48,32},{64,48},{80,64},{96,80},{112,96},{0,112},{1... | collective-permute-start | bytes 49160 | tf_op jit(solution)/shard_map/ppermute | solution.py:20
  40.9 10.5 %collective-permute-start.2 = (f32[32,98,1]{1,0,2:T(8,128)}, f32[32,98,1]{1,0,2:T(8,128)}, u32[]{:S(2)}, u32[]{:S(2)}) collective-permute-start(f32[32,98,1]{1,0,2:T(8,128)} %copy.185), channel_id=1, source_target_pairs={{0,1},{1,2},{2,3},{3,4},{4,5},{5,6},{6,7},{7,8},{8,9},{9,10},{10,1... | collective-permute-start | bytes 37640 | tf_op jit(solution)/shard_map/ppermute | solution.py:17
  50.7 3.6 %collective-permute-start.3 = (f32[32,98,1]{1,0,2:T(8,128)}, f32[32,98,1]{1,0,2:T(8,128)}, u32[]{:S(2)}, u32[]{:S(2)}) collective-permute-start(f32[32,98,1]{1,0,2:T(8,128)} %copy.186), channel_id=1, source_target_pairs={{1,0},{2,1},{3,2},{4,3},{5,4},{6,5},{7,6},{8,7},{9,8},{10,9},{11,1... | collective-permute-start | bytes 37640 | tf_op jit(solution)/shard_map/ppermute | solution.py:20
  63.9 2.5 copy-start.2
  64.4 3.6 %copy-start.9 = (f32[20,6,2047]{2,0,1:T(8,128)}, f32[20,6,2047]{2,0,1:T(8,128)S(1)}, u32[]{:S(2)}) copy-start(f32[20,6,2047]{2,0,1:T(8,128)S(1)} %get-tuple-element.68) | copy-start | bytes 2947684
  64.4 3.6 %copy-start.7 = (f32[20,6,2047]{2,0,1:T(8,128)}, f32[20,6,2047]{2,0,1:T(8,128)S(1)}, u32[]{:S(2)}) copy-start(f32[20,6,2047]{2,0,1:T(8,128)S(1)} %get-tuple-element.67) | copy-start | bytes 2947684
  69.5 2.4 copy-start.15
  74.6 9.4 %copy-start = (f32[20,6,2048]{2,0,1:T(8,128)}, f32[20,6,2048]{2,0,1:T(8,128)S(1)}, u32[]{:S(2)}) copy-start(f32[20,6,2048]{2,0,1:T(8,128)S(1)} %slice.244) | copy-start | bytes 2949124
  89.6 2.4 copy-start.8
  100.6 2.4 copy-start.1
  105.6 3.9 %copy-start.13 = (f32[20,6,2048]{2,0,1:T(8,128)}, f32[20,6,2048]{2,0,1:T(8,128)S(1)}, u32[]{:S(2)}) copy-start(f32[20,6,2048]{2,0,1:T(8,128)S(1)} %convolution_bitcast_fusion.6) | copy-start | bytes 2949124
  109.8 2.9 copy-start.12
  112.7 3.2 %copy-start.34 = (f32[98]{0:T(128)S(1)}, f32[98]{0:T(128)}, u32[]{:S(2)}) copy-start(f32[98]{0:T(128)} %and_convert_fusion) | copy-start | bytes 1180
  115.9 3.9 %copy-start.14 = (f32[20,6,2048]{2,0,1:T(8,128)S(1)}, f32[20,6,2048]{2,0,1:T(8,128)}, u32[]{:S(2)}) copy-start(f32[20,6,2048]{2,0,1:T(8,128)} %convolution_bitcast_fusion.8) | copy-start | bytes 2949124
  115.9 3.9 %slice-start.1 = ((f32[20,6,2048]{2,0,1:T(8,128)}), f32[20,6,1]{2,0,1:T(8,128)S(1)}, s32[]{:S(2)}) async-start(f32[20,6,2048]{2,0,1:T(8,128)} %copy-done.13), calls=%async_computation.4 | async-start | bytes 147456 | tf_op jit(solution)/shard_map/transpose(jvp(jit(_roll_static)))/split | solution.py:56
  127.7 19.5 %copy-start.4 = (f32[32,98,130]{2,1,0:T(8,128)S(1)}, f32[32,98,130]{2,1,0:T(8,128)}, u32[]{:S(2)}) copy-start(f32[32,98,130]{2,1,0:T(8,128)} %pad_maximum_fusion) | copy-start | bytes 4892164
  132.8 166.6 %all-to-all-start.1 = ((f32[16,20,6,128]{3,1,2,0:T(8,128)}), f32[16,20,6,128]{3,1,2,0:T(8,128)}, u32[]{:S(2)}, u32[]{:S(2)}) async-start(f32[16,20,6,128]{3,1,2,0:T(8,128)} %fusion.47), calls=%async_computation.1 | async-start | bytes 2359296 | tf_op jit(solution)/shard_map/all_to_all | solution.py:125
  147.2 148.6 %all-reduce.24.cloned.1.call-start = ((), (), s32[]{:S(2)}) async-start(), calls=%async_computation.2 | async-start | bytes 131072 | tf_op jit(solution)/shard_map/psum | solution.py:123
  153.1 6.2 %collective-permute-start.4 = (f32[10,1,128]{2,1,0:T(1,128)S(1)}, f32[10,1,128]{2,1,0:T(1,128)S(1)}, u32[]{:S(2)}, u32[]{:S(2)}) collective-permute-start(f32[10,1,128]{2,1,0:T(1,128)S(1)} %get-tuple-element.74), channel_id=1, source_target_pairs={{0,16},{16,32},{32,48},{48,64},{64,80},{80,96},{96,112},{112,0},{1... | collective-permute-start | bytes 15368 | tf_op jit(solution)/shard_map/ppermute | solution.py:17
  153.2 6.1 %collective-permute-start.5 = (f32[10,1,128]{2,1,0:T(1,128)S(1)}, f32[10,1,128]{2,1,0:T(1,128)S(1)}, u32[]{:S(2)}, u32[]{:S(2)}) collective-permute-start(f32[10,1,128]{2,1,0:T(1,128)S(1)} %get-tuple-element.73), channel_id=1, source_target_pairs={{16,0},{32,16},{48,32},{64,48},{80,64},{96,80},{112,96},{0,112},{1... | collective-permute-start | bytes 15368 | tf_op jit(solution)/shard_map/ppermute | solution.py:20
  162.8 6.3 %collective-permute-start.6 = (f32[10,98,1]{1,2,0:T(1,128)S(1)}, f32[10,98,1]{1,2,0:T(1,128)S(1)}, u32[]{:S(2)}, u32[]{:S(2)}) collective-permute-start(f32[10,98,1]{1,2,0:T(1,128)S(1)} %copy.196), channel_id=1, source_target_pairs={{1,0},{2,1},{3,2},{4,3},{5,4},{6,5},{7,6},{8,7},{9,8},{10,9},{11,1... | collective-permute-start | bytes 11768 | tf_op jit(solution)/shard_map/ppermute | solution.py:20
  165.9 4.3 %collective-permute-start.7 = (f32[10,98,1]{1,2,0:T(1,128)S(1)}, f32[10,98,1]{1,2,0:T(1,128)S(1)}, u32[]{:S(2)}, u32[]{:S(2)}) collective-permute-start(f32[10,98,1]{1,2,0:T(1,128)S(1)} %copy.198), channel_id=1, source_target_pairs={{0,1},{1,2},{2,3},{3,4},{4,5},{5,6},{6,7},{7,8},{8,9},{9,10},{10,1... | collective-permute-start | bytes 11768 | tf_op jit(solution)/shard_map/ppermute | solution.py:17
  (24 other events, 38.1 us)
Sparse Core Ops, SparseCore 0:
  158.4 137.3 all-reduce.23
